TPU v7x, 256 devices: a whole 4x4x8 slice. The times are simulated.
256 devices in a mesh: expert: 128 (over z, x, y), dp: 2 (over core).
Axes of the slice: x: 4, y: 4, z: 8, core: 2. Of those that a mesh axis runs over, the one named last changes fastest.
Arguments:
- hidden: bfloat16 [32768, 8, 1024], P(('expert', 'dp')), may hold values from -8 to 8
- routes: int32 [32768, 8], P(('expert', 'dp')), may hold values from 0 to 127, as said below
- slots: int32 [32768, 8], P(('expert', 'dp')), may hold values from 0 to 15, as said below
- down_weight: bfloat16 [128, 1024, 7168], P('expert', None, 'dp'), may hold values from -0.1875 to 0.1875
- omega: bfloat16 [128, 1024, 256], P('expert'), may hold values from -0.1875 to 0.1875
Outputs:
- whitening: float32 [128, 1024, 1024], P('expert', 'dp')
- basis: float32 [2, 3584, 256], P('dp', 'expert')
Inputs may be any that keep to these rules, and one draw needn't show every extreme that they name: `routes`: each token names 8 different experts. Among the tokens of one device no expert is named more than 16 times, and one expert is named exactly 16 times by the tokens of every device. Among the tokens of one device, the pairs that name one expert have different slots.
All inputs are finite; a program needn't handle non-finite values.
Results may differ from a plain program's by a relative error of at most 0.0032.
Values may be sent and summed in bfloat16 or wider, within the bound.
No kernel may reach another device: no remote copies, remote signals or barrier semaphores. Data moves between devices by JAX's collectives and lax.ppermute only.
A program may use at most 128 MiB of HBM per device.

v0:
```python
import math
import jax
import jax.numpy as jnp
from jax import lax
from jax.sharding import PartitionSpec as P

damping = 0.1
jitter = 1e-06


def contract(left, right):
    return lax.dot_general(
        left, right, (((0,), (0,)), ((), ())), preferred_element_type=jnp.float32
    )


def local(hidden, routes, slots, down_weight, omega):
    n_exp = lax.axis_size("expert")
    n_dp = lax.axis_size("dp")
    tok_rows, n_route, hid_width = hidden.shape
    capacity = 2 * tok_rows * n_route // n_exp
    n_slot = n_exp * n_dp * capacity
    slot_index = (routes * capacity + slots).reshape(-1)
    outgoing = jnp.zeros((n_exp * capacity, hid_width), jnp.bfloat16)
    outgoing = (
        outgoing.at[slot_index]
        .set(hidden.reshape(-1, hid_width))
        .reshape(n_exp, capacity, hid_width)
    )
    received = lax.all_to_all(outgoing, "expert", split_axis=0, concat_axis=0, tiled=True).reshape(
        n_exp * capacity, hid_width
    )
    gram_mat = lax.psum(contract(received, received), "dp") / n_slot
    identity_mat = jnp.eye(hid_width, dtype=jnp.float32)
    damped = gram_mat + (damping * jnp.mean(jnp.diagonal(gram_mat)) + jitter) * identity_mat
    whitening = jnp.linalg.cholesky(damped)
    test_mat = jnp.dot(
        whitening, omega[0].astype(jnp.float32), precision=lax.Precision.HIGHEST
    ).astype(jnp.bfloat16)
    down_half = down_weight[0]
    half_cols = down_half.shape[1]
    row_share = half_cols // n_exp
    whole_half = lax.psum(contract(down_half, test_mat), "expert")
    small_gram = lax.psum(jnp.dot(whole_half.T, whole_half, precision=lax.Precision.HIGHEST), "dp")
    sketch = lax.dynamic_slice_in_dim(
        whole_half, lax.axis_index("expert") * row_share, row_share, 0
    )
    qr_factor = jnp.linalg.cholesky(small_gram)
    basis_rows = jax.scipy.linalg.solve_triangular(qr_factor, sketch.T, lower=True).T * math.sqrt(
        half_cols * n_dp
    )
    own_rows = lax.dynamic_slice_in_dim(
        whitening, lax.axis_index("dp") * (hid_width // n_dp), hid_width // n_dp, 0
    )
    return (own_rows[None], basis_rows[None])


def solution(mesh):
    placed = (
        P(("expert", "dp"), None, None),
        P(("expert", "dp"), None),
        P(("expert", "dp"), None),
        P("expert", None, "dp"),
        P("expert", None, None),
    )
    return jax.shard_map(
        local,
        mesh=mesh,
        in_specs=placed,
        out_specs=(P("expert", "dp", None), P("dp", "expert", None)),
        check_vma=False,
    )
```

profile of v0, /device:TPU:1, one launch (start us, length us, event | category | flops | bytes accessed | tf_op | source)
XLA Modules:
  0.0 775.2 jit_solution(16030494886946830001)
XLA Ops:
  8.8 7.9 %scatter_custom_fusion = bf16[2048,1024]{1,0:T(8,128)(2,1)} fusion(s32[1024]{0:T(1024)S(1)} %bitcast.111, bf16[128,8,1024]{2,1,0:T(8,128)(2,1)S(1)} %copy-done, bf16[]{:T(256)} %constant.347.clone.1), kind=kCustom, calls=%fused_computation.14 | custom fusion | bytes 6291458 | tf_op jit(solution)/shard_map/scatter | solution.py:27
  16.7 110.1 %all_to_all.5 = bf16[128,16,1024]{2,1,0:T(8,128)(2,1)S(1)} all-to-all(bf16[128,16,1024]{2,1,0:T(8,128)(2,1)} %bitcast.109), channel_id=1, replica_groups=mesh['expert'=128,'dp'=2] {'expert'}, dimensions={0} | all-to-all | bytes 8388608 | tf_op jit(solution)/shard_map/all_to_all | solution.py:30
  126.7 6.2 convolution_bitcast_fusion
  133.0 38.1 %all-reduce.6.cloned.1.call-done = f32[1024,1024]{0,1:T(8,128)} async-done(((f32[1024,1024]{0,1:T(8,128)}), f32[1024,1024]{0,1:T(8,128)}) %all-reduce.6.cloned.1.call-update) | async-done | bytes 4194320 | tf_op jit(solution)/shard_map/psum | solution.py:33
  171.2 5.0 broadcast_multiply_fusion
  176.2 16.8 %gather_fusion = f32[1024]{0:T(1024)S(1)} fusion(f32[1024,1024]{0,1:T(8,128)} %broadcast_multiply_fusion, s32[1024]{0:T(1024)S(1)} %bitcast.108), kind=kCustom, calls=%fused_computation | custom fusion | bytes 16384 | tf_op jit(solution)/shard_map/jit(diagonal)/cond/branch_0_fun/gather | solution.py:35
  194.3 5.0 select_add_fusion
  199.3 5.5 copy.56
  204.8 4.5 fusion.5
  209.3 1.9 copy-done.3
  211.2 11.7 %cholesky.249 = f32[128,128]{1,0:T(8,128)S(1)} custom-call(f32[128,128]{1,0:T(8,128)S(1)} %cholesky.650), custom_call_target="Cholesky" | custom-call | tf_op jit(solution)/shard_map/jit(cholesky)/cholesky | solution.py:36
  223.0 9.8 %custom-call.67 = f32[1,128,128]{1,2,0:T(8,128)S(1)} custom-call(f32[1,128,128]{2,1,0:T(8,128)S(1)} %get-tuple-element.44), custom_call_target="InvertDiagBlocksLowerTriangular" | custom-call | tf_op jit(solution)/shard_map/jit(cholesky)/cholesky | solution.py:36
  232.9 1.5 fusion.17
  234.6 1.6 convolution_subtract_fusion
  236.2 11.7 %cholesky.274 = f32[128,128]{1,0:T(8,128)S(1)} custom-call(f32[128,128]{1,0:T(8,128)S(1)} %cholesky.654), custom_call_target="Cholesky" | custom-call | tf_op jit(solution)/shard_map/jit(cholesky)/cholesky | solution.py:36
  248.2 2.5 cholesky.281
  250.7 9.8 %custom-call.68 = f32[1,128,128]{1,2,0:T(8,128)S(1)} custom-call(f32[1,128,128]{2,1,0:T(8,128)S(1)} %get-tuple-element.42), custom_call_target="InvertDiagBlocksLowerTriangular" | custom-call | tf_op jit(solution)/shard_map/jit(cholesky)/cholesky | solution.py:36
  263.3 2.7 convolution_subtract_fusion.1
  266.0 11.7 %cholesky.299 = f32[128,128]{1,0:T(8,128)S(1)} custom-call(f32[128,128]{1,0:T(8,128)S(1)} %cholesky.659), custom_call_target="Cholesky" | custom-call | tf_op jit(solution)/shard_map/jit(cholesky)/cholesky | solution.py:36
  278.5 9.8 %custom-call.69 = f32[1,128,128]{1,2,0:T(8,128)S(1)} custom-call(f32[1,128,128]{2,1,0:T(8,128)S(1)} %get-tuple-element.40), custom_call_target="InvertDiagBlocksLowerTriangular" | custom-call | tf_op jit(solution)/shard_map/jit(cholesky)/cholesky | solution.py:36
  289.6 3.5 convolution_subtract_fusion.2
  293.1 11.7 %cholesky.539 = f32[128,128]{1,0:T(8,128)S(1)} custom-call(f32[128,128]{1,0:T(8,128)S(1)} %cholesky.664), custom_call_target="Cholesky" | custom-call | tf_op jit(solution)/shard_map/jit(cholesky)/cholesky | solution.py:36
  305.6 9.8 %custom-call.70 = f32[1,128,128]{1,2,0:T(8,128)S(1)} custom-call(f32[1,128,128]{2,1,0:T(8,128)S(1)} %get-tuple-element.38), custom_call_target="InvertDiagBlocksLowerTriangular" | custom-call | tf_op jit(solution)/shard_map/jit(cholesky)/cholesky | solution.py:36
  316.5 3.1 convolution_subtract_fusion.3
  319.7 11.8 %cholesky.558 = f32[128,128]{1,0:T(8,128)S(1)} custom-call(f32[128,128]{1,0:T(8,128)S(1)} %cholesky.669), custom_call_target="Cholesky" | custom-call | tf_op jit(solution)/shard_map/jit(cholesky)/cholesky | solution.py:36
  332.3 9.8 %custom-call.71 = f32[1,128,128]{1,2,0:T(8,128)S(1)} custom-call(f32[1,128,128]{2,1,0:T(8,128)S(1)} %get-tuple-element.36), custom_call_target="InvertDiagBlocksLowerTriangular" | custom-call | tf_op jit(solution)/shard_map/jit(cholesky)/cholesky | solution.py:36
  343.3 3.1 convolution_subtract_fusion.4
  346.4 11.7 %cholesky.578 = f32[128,128]{1,0:T(8,128)S(1)} custom-call(f32[128,128]{1,0:T(8,128)S(1)} %cholesky.674), custom_call_target="Cholesky" | custom-call | tf_op jit(solution)/shard_map/jit(cholesky)/cholesky | solution.py:36
  358.8 9.8 %custom-call.72 = f32[1,128,128]{1,2,0:T(8,128)S(1)} custom-call(f32[1,128,128]{2,1,0:T(8,128)S(1)} %get-tuple-element.34), custom_call_target="InvertDiagBlocksLowerTriangular" | custom-call | tf_op jit(solution)/shard_map/jit(cholesky)/cholesky | solution.py:36
  369.6 2.9 convolution_subtract_fusion.5
  372.5 11.7 %cholesky.598 = f32[128,128]{1,0:T(8,128)S(1)} custom-call(f32[128,128]{1,0:T(8,128)S(1)} %cholesky.679), custom_call_target="Cholesky" | custom-call | tf_op jit(solution)/shard_map/jit(cholesky)/cholesky | solution.py:36
  385.0 9.8 %custom-call.77 = f32[1,128,128]{1,2,0:T(8,128)S(1)} custom-call(f32[1,128,128]{2,1,0:T(8,128)S(1)} %get-tuple-element.32), custom_call_target="InvertDiagBlocksLowerTriangular" | custom-call | tf_op jit(solution)/shard_map/jit(cholesky)/cholesky/custom-call.17 | solution.py:36
  395.8 2.1 convolution_subtract_fusion.8
  397.9 11.7 %cholesky.612 = f32[128,128]{1,0:T(8,128)S(1)} custom-call(f32[128,128]{1,0:T(8,128)S(1)} %convolution_subtract_fusion.8), custom_call_target="Cholesky" | custom-call | tf_op jit(solution)/shard_map/jit(cholesky)/cholesky | solution.py:36
  420.0 2.7 select_select_fusion
  422.8 1.9 copy-done.2
  424.7 3.8 convolution_convert_fusion
  428.6 7.1 fusion.2
  435.8 229.8 %all-reduce.8.cloned.1.call-done = f32[3584,256]{0,1:T(8,128)} async-done(((f32[3584,256]{0,1:T(8,128)}), f32[3584,256]{0,1:T(8,128)}) %all-reduce.8.cloned.1.call-update) | async-done | bytes 3670032 | tf_op jit(solution)/shard_map/psum | solution.py:43
  665.6 7.0 fusion.47
  672.6 3.3 constant_dynamic-slice_fusion.1
  675.9 3.0 copy.71
  680.0 24.5 %all-reduce.10.cloned.1.call-done = f32[256,256]{0,1:T(8,128)} async-done(((f32[256,256]{0,1:T(8,128)}), f32[256,256]{0,1:T(8,128)}) %all-reduce.10.cloned.1.call-update) | async-done | bytes 262160 | tf_op jit(solution)/shard_map/psum | solution.py:44
  706.6 11.7 %cholesky.625 = f32[128,128]{1,0:T(8,128)S(1)} custom-call(f32[128,128]{1,0:T(8,128)S(1)} %cholesky.683), custom_call_target="Cholesky" | custom-call | tf_op jit(solution)/shard_map/jit(cholesky)/cholesky | solution.py:48
  718.4 9.8 %custom-call.78 = f32[1,128,128]{1,2,0:T(8,128)S(1)} custom-call(f32[1,128,128]{2,1,0:T(8,128)S(1)} %get-tuple-element.30), custom_call_target="InvertDiagBlocksLowerTriangular" | custom-call | tf_op jit(solution)/shard_map/jit(cholesky)/cholesky/custom-call.17 | solution.py:48
  728.7 11.7 %cholesky.634 = f32[128,128]{1,0:T(8,128)S(1)} custom-call(f32[128,128]{1,0:T(8,128)S(1)} %convolution_subtract_fusion.7), custom_call_target="Cholesky" | custom-call | tf_op jit(solution)/shard_map/jit(cholesky)/cholesky | solution.py:48
  743.1 4.1 while.1
  747.2 19.9 %custom-call.73 = f32[2,128,128]{1,2,0:T(8,128)S(1)} custom-call(f32[2,128,128]{2,1,0:T(8,128)S(1)} %get-tuple-element.10), custom_call_target="InvertDiagBlocksLowerTriangular" | custom-call | tf_op jit(solution)/shard_map/jit(_solve_triangular)/triangular_solve | solution.py:49
  (91 shorter events, 31.0 us)
Async XLA Ops:
  7.2 1.6 copy-start
  7.2 164.0 %all-reduce.6.cloned.1.call-start = ((), (), s32[]{:S(2)}) async-start(), calls=%async_computation.1 | async-start | bytes 8388608 | tf_op jit(solution)/shard_map/psum | solution.py:33
  133.0 532.6 %all-reduce.8.cloned.1.call-start = ((), (), s32[]{:S(2)}) async-start(), calls=%async_computation.2 | async-start | bytes 7340032 | tf_op jit(solution)/shard_map/psum | solution.py:43
  209.3 1.9 copy-start.3
  420.0 4.7 copy-start.4
  422.8 1.9 copy-start.2
  435.7 268.8 %all-reduce.10.cloned.1.call-start = ((), (), s32[]{:S(2)}) async-start(), calls=%async_computation.3 | async-start | bytes 524288 | tf_op jit(solution)/shard_map/psum | solution.py:44
  672.6 95.9 %copy-start.1 = (bf16[128,8,1024]{2,1,0:T(8,128)(2,1)S(1)}, bf16[128,8,1024]{2,1,0:T(8,128)(2,1)}, u32[]{:S(2)}) copy-start(bf16[128,8,1024]{2,1,0:T(8,128)(2,1)} %param.7) | copy-start | bytes 6291460
Sparse Core Ops, SparseCore 0:
  133.1 38.0 all-reduce.5
  435.8 229.7 all-reduce.7
  672.7 31.7 all-reduce.9
where the time goes:
time: 784 us; the launch traced here: 775 us
  waiting for transfers between devices  293 us (37%)
  other arithmetic  242 us (31%)
  blocking collectives  110 us (14%)
  local copies, waits for them, and re-layouts  57 us (7%)
  matrix products  52.5 us (7%)
  between operations  21.4 us (3%)
    psum x1, waiting for transfers between devices, local(): whole_half = lax.psum(contract(down_half, test_mat), 'expert')  230 us
    another operation x30, other arithmetic, local(): whitening = jnp.linalg.cholesky(damped)  167 us
    all_to_all x1, blocking collectives, local(): lax.all_to_all(outgoing, 'expert', split_axis=0, concat_axis=0, tiled=True)  110 us
    psum x1, waiting for transfers between devices, local(): gram_mat = lax.psum(contract(received, received), 'dp') / n_slot  38.1 us
    another operation x7, other arithmetic, local(): qr_factor = jnp.linalg.cholesky(small_gram)  34.6 us
    another operation x14, matrix products, local(): whitening = jnp.linalg.cholesky(damped)  27.2 us
    psum x1, waiting for transfers between devices, local(): lax.psum(jnp.dot(whole_half.T, whole_half, precision=lax.Precision.HIGHES...  24.5 us
    another operation x3, other arithmetic, local(): jax.scipy.linalg.solve_triangular(qr_factor, sketch.T, lower=True)  19.9 us
  transfers between devices with their start and end apart: 3, of which 3 were waited for; matrix products, arithmetic and copies ran while one was open for 1% of the time, Pallas kernels for 0%

commit v1 on v0

--- a/solution.py
+++ b/solution.py
@@ -1,3 +1,4 @@
+import functools
 import math
 import jax
 import jax.numpy as jnp
@@ -6,6 +7,13 @@
 
 damping = 0.1
 jitter = 1e-06
+
+
+def return_all_core(z_in, named_axis):
+    return jnp.sum(lax.all_gather(z_in, named_axis), axis=0)
+
+
+squares_draft = functools.partial(return_all_core, named_axis="dp")
 
 
 def contract(left, right):
@@ -41,7 +49,7 @@
     half_cols = down_half.shape[1]
     row_share = half_cols // n_exp
     whole_half = lax.psum(contract(down_half, test_mat), "expert")
-    small_gram = lax.psum(jnp.dot(whole_half.T, whole_half, precision=lax.Precision.HIGHEST), "dp")
+    small_gram = squares_draft(jnp.dot(whole_half.T, whole_half, precision=lax.Precision.HIGHEST))
     sketch = lax.dynamic_slice_in_dim(
         whole_half, lax.axis_index("expert") * row_share, row_share, 0
     )

time: 784 us -> 758 us (0.967)
  waiting for transfers between devices: 293 us -> 264 us
    psum x1 -> x0, waiting for transfers between devices: 24.5 us -> none  [local(): lax.psum(jnp.dot(whole_half.T, whole_half, precision=lax.Precision.HIGHES...]
  transfers between devices with their start and end apart: 3 -> 2, of which waited for: 3 -> 2; matrix products, arithmetic and copies ran while one was open for 1% -> 0% of each run, Pallas kernels for 0% -> 0%
where the time goes in v1:
time: 758 us; the launch traced here: 749 us
  waiting for transfers between devices  264 us (35%)
  other arithmetic  241 us (32%)
  blocking collectives  117 us (15%)
  local copies, waits for them, and re-layouts  53.3 us (7%)
  matrix products  51.9 us (7%)
  between operations  21.7 us (3%)
    psum x1, waiting for transfers between devices, local(): whole_half = lax.psum(contract(down_half, test_mat), 'expert')  226 us
    another operation x30, other arithmetic, local(): whitening = jnp.linalg.cholesky(damped)  167 us
    all_to_all x1, blocking collectives, local(): lax.all_to_all(outgoing, 'expert', split_axis=0, concat_axis=0, tiled=True)  110 us
    psum x1, waiting for transfers between devices, local(): gram_mat = lax.psum(contract(received, received), 'dp') / n_slot  38.1 us
    another operation x7, other arithmetic, local(): qr_factor = jnp.linalg.cholesky(small_gram)  34.7 us
    another operation x14, matrix products, local(): whitening = jnp.linalg.cholesky(damped)  27.2 us
    another operation x3, other arithmetic, local(): jax.scipy.linalg.solve_triangular(qr_factor, sketch.T, lower=True)  19.7 us
    gather x1, local copies, waits for them, and re-layouts, local(): jnp.diagonal(gram_mat)  16.8 us
  transfers between devices with their start and end apart: 2, of which 2 were waited for; matrix products, arithmetic and copies ran while one was open for 0% of the time, Pallas kernels for 0%

profile of v1, /device:TPU:1, one launch (start us, length us, event | category | flops | bytes accessed | tf_op | source)
XLA Modules:
  0.0 749.3 jit_solution(12923769956063512872)
XLA Ops:
  8.8 7.9 %scatter_custom_fusion = bf16[2048,1024]{1,0:T(8,128)(2,1)} fusion(s32[1024]{0:T(1024)S(1)} %bitcast.113, bf16[128,8,1024]{2,1,0:T(8,128)(2,1)S(1)} %copy-done, bf16[]{:T(256)} %constant.347.clone.1), kind=kCustom, calls=%fused_computation.14 | custom fusion | bytes 6291458 | tf_op jit(solution)/shard_map/scatter | solution.py:35
  16.7 110.1 %all_to_all.5 = bf16[128,16,1024]{2,1,0:T(8,128)(2,1)S(1)} all-to-all(bf16[128,16,1024]{2,1,0:T(8,128)(2,1)} %bitcast.110), channel_id=1, replica_groups=mesh['expert'=128,'dp'=2] {'expert'}, dimensions={0} | all-to-all | bytes 8388608 | tf_op jit(solution)/shard_map/all_to_all | solution.py:38
  126.7 6.2 convolution_bitcast_fusion
  133.0 38.1 %all-reduce.5.cloned.1.call-done = f32[1024,1024]{0,1:T(8,128)} async-done(((f32[1024,1024]{0,1:T(8,128)}), f32[1024,1024]{0,1:T(8,128)}) %all-reduce.5.cloned.1.call-update) | async-done | bytes 4194320 | tf_op jit(solution)/shard_map/psum | solution.py:41
  171.2 5.0 broadcast_multiply_fusion
  176.2 16.8 %gather_fusion = f32[1024]{0:T(1024)S(1)} fusion(f32[1024,1024]{0,1:T(8,128)} %broadcast_multiply_fusion, s32[1024]{0:T(1024)S(1)} %bitcast.109), kind=kCustom, calls=%fused_computation | custom fusion | bytes 16384 | tf_op jit(solution)/shard_map/jit(diagonal)/cond/branch_0_fun/gather | solution.py:43
  194.3 5.0 select_add_fusion
  199.3 5.5 copy.54
  204.8 4.5 fusion.5
  209.3 1.9 copy-done.3
  211.2 11.7 %cholesky.249 = f32[128,128]{1,0:T(8,128)S(1)} custom-call(f32[128,128]{1,0:T(8,128)S(1)} %cholesky.650), custom_call_target="Cholesky" | custom-call | tf_op jit(solution)/shard_map/jit(cholesky)/cholesky | solution.py:44
  223.0 9.8 %custom-call.67 = f32[1,128,128]{1,2,0:T(8,128)S(1)} custom-call(f32[1,128,128]{2,1,0:T(8,128)S(1)} %get-tuple-element.44), custom_call_target="InvertDiagBlocksLowerTriangular" | custom-call | tf_op jit(solution)/shard_map/jit(cholesky)/cholesky | solution.py:44
  232.9 1.5 fusion.17
  234.6 1.6 convolution_subtract_fusion
  236.2 11.7 %cholesky.274 = f32[128,128]{1,0:T(8,128)S(1)} custom-call(f32[128,128]{1,0:T(8,128)S(1)} %cholesky.654), custom_call_target="Cholesky" | custom-call | tf_op jit(solution)/shard_map/jit(cholesky)/cholesky | solution.py:44
  248.2 2.5 cholesky.281
  250.7 9.8 %custom-call.68 = f32[1,128,128]{1,2,0:T(8,128)S(1)} custom-call(f32[1,128,128]{2,1,0:T(8,128)S(1)} %get-tuple-element.42), custom_call_target="InvertDiagBlocksLowerTriangular" | custom-call | tf_op jit(solution)/shard_map/jit(cholesky)/cholesky | solution.py:44
  263.3 2.7 convolution_subtract_fusion.1
  266.0 11.7 %cholesky.299 = f32[128,128]{1,0:T(8,128)S(1)} custom-call(f32[128,128]{1,0:T(8,128)S(1)} %cholesky.659), custom_call_target="Cholesky" | custom-call | tf_op jit(solution)/shard_map/jit(cholesky)/cholesky | solution.py:44
  278.5 9.8 %custom-call.69 = f32[1,128,128]{1,2,0:T(8,128)S(1)} custom-call(f32[1,128,128]{2,1,0:T(8,128)S(1)} %get-tuple-element.40), custom_call_target="InvertDiagBlocksLowerTriangular" | custom-call | tf_op jit(solution)/shard_map/jit(cholesky)/cholesky | solution.py:44
  289.6 3.5 convolution_subtract_fusion.2
  293.1 11.7 %cholesky.539 = f32[128,128]{1,0:T(8,128)S(1)} custom-call(f32[128,128]{1,0:T(8,128)S(1)} %cholesky.664), custom_call_target="Cholesky" | custom-call | tf_op jit(solution)/shard_map/jit(cholesky)/cholesky | solution.py:44
  305.6 9.8 %custom-call.70 = f32[1,128,128]{1,2,0:T(8,128)S(1)} custom-call(f32[1,128,128]{2,1,0:T(8,128)S(1)} %get-tuple-element.38), custom_call_target="InvertDiagBlocksLowerTriangular" | custom-call | tf_op jit(solution)/shard_map/jit(cholesky)/cholesky | solution.py:44
  316.5 3.1 convolution_subtract_fusion.3
  319.7 11.8 %cholesky.558 = f32[128,128]{1,0:T(8,128)S(1)} custom-call(f32[128,128]{1,0:T(8,128)S(1)} %cholesky.669), custom_call_target="Cholesky" | custom-call | tf_op jit(solution)/shard_map/jit(cholesky)/cholesky | solution.py:44
  332.3 9.8 %custom-call.71 = f32[1,128,128]{1,2,0:T(8,128)S(1)} custom-call(f32[1,128,128]{2,1,0:T(8,128)S(1)} %get-tuple-element.36), custom_call_target="InvertDiagBlocksLowerTriangular" | custom-call | tf_op jit(solution)/shard_map/jit(cholesky)/cholesky | solution.py:44
  343.3 3.1 convolution_subtract_fusion.4
  346.4 11.7 %cholesky.578 = f32[128,128]{1,0:T(8,128)S(1)} custom-call(f32[128,128]{1,0:T(8,128)S(1)} %cholesky.674), custom_call_target="Cholesky" | custom-call | tf_op jit(solution)/shard_map/jit(cholesky)/cholesky | solution.py:44
  358.8 9.8 %custom-call.72 = f32[1,128,128]{1,2,0:T(8,128)S(1)} custom-call(f32[1,128,128]{2,1,0:T(8,128)S(1)} %get-tuple-element.34), custom_call_target="InvertDiagBlocksLowerTriangular" | custom-call | tf_op jit(solution)/shard_map/jit(cholesky)/cholesky | solution.py:44
  369.6 2.9 convolution_subtract_fusion.5
  372.5 11.7 %cholesky.598 = f32[128,128]{1,0:T(8,128)S(1)} custom-call(f32[128,128]{1,0:T(8,128)S(1)} %cholesky.679), custom_call_target="Cholesky" | custom-call | tf_op jit(solution)/shard_map/jit(cholesky)/cholesky | solution.py:44
  385.0 9.8 %custom-call.77 = f32[1,128,128]{1,2,0:T(8,128)S(1)} custom-call(f32[1,128,128]{2,1,0:T(8,128)S(1)} %get-tuple-element.32), custom_call_target="InvertDiagBlocksLowerTriangular" | custom-call | tf_op jit(solution)/shard_map/jit(cholesky)/cholesky/custom-call.17 | solution.py:44
  395.8 2.1 convolution_subtract_fusion.8
  397.9 11.7 %cholesky.612 = f32[128,128]{1,0:T(8,128)S(1)} custom-call(f32[128,128]{1,0:T(8,128)S(1)} %convolution_subtract_fusion.8), custom_call_target="Cholesky" | custom-call | tf_op jit(solution)/shard_map/jit(cholesky)/cholesky | solution.py:44
  420.0 2.7 select_select_fusion
  422.8 1.9 copy-done.2
  424.7 3.8 convolution_convert_fusion
  428.6 7.1 fusion.2
  435.7 1.8 constant_dynamic-slice_fusion.1
  437.5 1.8 copy.69
  439.3 226.3 %all-reduce.7.cloned.1.call-done = f32[3584,256]{0,1:T(8,128)} async-done(((f32[3584,256]{0,1:T(8,128)}), f32[3584,256]{0,1:T(8,128)}) %all-reduce.7.cloned.1.call-update) | async-done | bytes 3670032 | tf_op jit(solution)/shard_map/psum | solution.py:51
  665.6 6.4 fusion.47
  672.0 7.0 all-gather
  679.2 11.7 %cholesky.625 = f32[128,128]{1,0:T(8,128)S(1)} custom-call(f32[128,128]{1,0:T(8,128)S(1)} %cholesky.683), custom_call_target="Cholesky" | custom-call | tf_op jit(solution)/shard_map/jit(cholesky)/cholesky | solution.py:56
  691.0 9.8 %custom-call.78 = f32[1,128,128]{1,2,0:T(8,128)S(1)} custom-call(f32[1,128,128]{2,1,0:T(8,128)S(1)} %get-tuple-element.30), custom_call_target="InvertDiagBlocksLowerTriangular" | custom-call | tf_op jit(solution)/shard_map/jit(cholesky)/cholesky/custom-call.17 | solution.py:56
  701.3 11.7 %cholesky.634 = f32[128,128]{1,0:T(8,128)S(1)} custom-call(f32[128,128]{1,0:T(8,128)S(1)} %convolution_subtract_fusion.7), custom_call_target="Cholesky" | custom-call | tf_op jit(solution)/shard_map/jit(cholesky)/cholesky | solution.py:56
  715.8 4.3 while.1
  720.0 19.7 %custom-call.73 = f32[2,128,128]{1,2,0:T(8,128)S(1)} custom-call(f32[2,128,128]{2,1,0:T(8,128)S(1)} %get-tuple-element.10), custom_call_target="InvertDiagBlocksLowerTriangular" | custom-call | tf_op jit(solution)/shard_map/jit(_solve_triangular)/triangular_solve | solution.py:57
  (90 shorter events, 29.1 us)
Async XLA Ops:
  7.2 1.6 copy-start
  7.2 164.0 %all-reduce.5.cloned.1.call-start = ((), (), s32[]{:S(2)}) async-start(), calls=%async_computation.1 | async-start | bytes 8388608 | tf_op jit(solution)/shard_map/psum | solution.py:41
  133.0 532.6 %all-reduce.7.cloned.1.call-start = ((), (), s32[]{:S(2)}) async-start(), calls=%async_computation.2 | async-start | bytes 7340032 | tf_op jit(solution)/shard_map/psum | solution.py:51
  209.3 1.9 copy-start.3
  420.0 4.7 copy-start.4
  422.8 1.9 copy-start.2
  665.6 76.6 %copy-start.1 = (bf16[128,8,1024]{2,1,0:T(8,128)(2,1)S(1)}, bf16[128,8,1024]{2,1,0:T(8,128)(2,1)}, u32[]{:S(2)}) copy-start(bf16[128,8,1024]{2,1,0:T(8,128)(2,1)} %param.7) | copy-start | bytes 6291460
Sparse Core Ops, SparseCore 0:
  133.1 38.0 all-reduce.4
  435.8 229.7 all-reduce.6
